TPU v7x, 256 devices: a whole 4x4x8 slice. The times are simulated.
256 devices in a mesh: gx: 32 (over x, y, core), gy: 8 (over z).
Axes of the slice: x: 4, y: 4, z: 8, core: 2. Of those that a mesh axis runs over, the one named last changes fastest.
Arguments:
- leaf_load: bfloat16 [65536, 384], P(('gx', 'gy')), may hold values from -6 to 6
- front_zero: bfloat16 [65536, 8192], P(('gx', 'gy')), may hold values from -0.046875 to 0.046875
- front_one: bfloat16 [32768, 8192], P(('gx', 'gy')), may hold values from -0.046875 to 0.046875
- front_two: bfloat16 [16384, 8192], P(('gx', 'gy')), may hold values from -0.046875 to 0.046875
- front_root: bfloat16 [8192, 8192], P(('gx', 'gy')), may hold values from -0.046875 to 0.046875
- load_one: float32 [32768, 384], P(('gx', 'gy')), may hold values from -6 to 6
- load_two: float32 [16384, 384], P(('gx', 'gy')), may hold values from -6 to 6
- load_root: float32 [8192, 384], P(('gx', 'gy')), may hold values from -6 to 6
- map_one: int32 [8192, 2], replicated, may hold values from 0 to 255
- map_two: int32 [8192, 2], replicated, may hold values from 0 to 127
- map_root: int32 [8192, 2], replicated, may hold values from 0 to 63
- adjoint: float32 [64, 128, 384], P('gx', 'gy'), may hold values from -6 to 6
Outputs:
- root_solution: float32 [8192, 384], P(('gx', 'gy'))
- gradient: float32 [64, 128, 384], P('gx', 'gy')
All inputs are finite; a program needn't handle non-finite values.
Results may differ from a plain program's by a relative error of at most 0.0055.
Values may be sent and summed in bfloat16 or wider, within the bound.
No kernel may reach another device: no remote copies, remote signals or barrier semaphores. Data moves between devices by JAX's collectives and lax.ppermute only.
A program may use at most 64 MiB of HBM per device.

v0:
```python
import jax
import jax.numpy as jnp
from jax import lax
from jax.sharding import PartitionSpec as P


def swapped(x, axis, distance):
    return lax.ppermute(x, axis, [(i, i ^ 1 << distance) for i in range(lax.axis_size(axis))])


def padded_2(cells, sides, width):
    for axis, dim in sides:
        count = lax.axis_size(axis)
        ends = count - 1
        head = lax.slice_in_dim(cells, 0, width, axis=dim)
        tail = lax.slice_in_dim(cells, cells.shape[dim] - width, cells.shape[dim], axis=dim)
        cells = jnp.concatenate(
            [
                lax.ppermute(tail, axis, [(i, (i + 1) % count) for i in range(ends)]),
                cells,
                lax.ppermute(head, axis, [((i + 1) % count, i) for i in range(ends)]),
            ],
            axis=dim,
        )
    return cells


def group_rows(values, bits):
    values = lax.all_gather(values, "gy", axis=0, tiled=True)
    column = lax.axis_index("gx")
    for bit in range(bits):
        other = swapped(values, "gx", bit)
        upper = column >> bit & 1 == 1
        values = jnp.where(
            upper, jnp.concatenate([other, values], 0), jnp.concatenate([values, other], 0)
        )
    return values


def local(
    leaf_load,
    front_zero,
    front_one,
    front_two,
    front_root,
    load_one,
    load_two,
    load_root,
    map_one,
    map_two,
    map_root,
    adjoint,
):
    leaf_bits = lax.axis_size("gx").bit_length() - 4
    fronts = (front_zero, front_one, front_two)
    loads = (load_one, load_two, load_root)
    mappings = (map_one, map_two, map_root)
    column = lax.axis_index("gx")
    row_index = lax.axis_index("gy")
    state = leaf_load
    for level in range(3):
        bits = leaf_bits + level
        whole = group_rows(state, bits)
        product = jnp.dot(fronts[level], whole, preferred_element_type=jnp.float32)
        other = swapped(product, "gx", bits)
        upper = column >> bits & 1 == 1
        first = jnp.where(upper, other, product)
        second = jnp.where(upper, product, other)
        half = product.shape[0] // 2
        position = column % 2 ** (bits + 1) * lax.axis_size("gy") + row_index
        local_map = lax.dynamic_slice_in_dim(mappings[level], position * half, half, 0)
        total = (
            loads[level]
            + jnp.take(first, local_map[:, 0], axis=0)
            + jnp.take(second, local_map[:, 1], axis=0)
        )
        state = total.astype(jnp.bfloat16)
    whole = group_rows(state, leaf_bits + 3)
    root_solution = jnp.dot(front_root, whole, preferred_element_type=jnp.float32)
    cells_x = adjoint.shape[0]
    cells_y = adjoint.shape[1]
    width = adjoint.shape[2]
    plane = root_solution.reshape(cells_x, cells_y, width)
    stacked = jnp.stack([plane, adjoint])
    padded = padded_2(stacked, (("gx", 1), ("gy", 2)), 1)
    padded_u = padded[0]
    padded_a = padded[1]
    gradient = jnp.zeros((cells_x, cells_y, width), jnp.float32)
    for lo_x, lo_y in ((2, 1), (0, 1), (1, 2), (1, 0)):
        near_u = padded_u[lo_x : lo_x + cells_x, lo_y : lo_y + cells_y]
        near_a = padded_a[lo_x : lo_x + cells_x, lo_y : lo_y + cells_y]
        gradient = gradient + (plane - near_u) * (adjoint - near_a)
    return (root_solution, gradient)


def solution(mesh):
    in_specs = (
        P(("gx", "gy"), None),
        P(("gx", "gy"), None),
        P(("gx", "gy"), None),
        P(("gx", "gy"), None),
        P(("gx", "gy"), None),
        P(("gx", "gy"), None),
        P(("gx", "gy"), None),
        P(("gx", "gy"), None),
        P(),
        P(),
        P(),
        P("gx", "gy", None),
    )
    out_specs = (P(("gx", "gy"), None), P("gx", "gy", None))
    return jax.shard_map(local, mesh=mesh, in_specs=in_specs, out_specs=out_specs, check_vma=False)
```

profile of v0, /device:TPU:34, one launch (start us, length us, event | category | flops | bytes accessed | tf_op | source)
XLA Modules:
  0.0 686.3 jit_solution(2727871176709467057)
XLA Ops:
  7.9 44.2 %all-gather.2.cloned.1.call-done = bf16[2048,384]{1,0:T(8,128)(2,1)} async-done(((bf16[256,384]{1,0:T(8,128)(2,1)}), bf16[2048,384]{1,0:T(8,128)(2,1)}) %all-gather.2.cloned.1.call-update) | async-done | bytes 1572880 | tf_op jit(solution)/shard_map/all_gather | solution.py:29
  55.8 5.5 maximum_select_fusion.8
  62.8 69.0 %collective-permute-done.1 = bf16[4096,384]{1,0:T(8,128)(2,1)} collective-permute-done((bf16[4096,384]{1,0:T(8,128)(2,1)}, bf16[4096,384]{1,0:T(8,128)(2,1)}, u32[]{:S(2)}, u32[]{:S(2)}) %collective-permute-start.1) | collective-permute-done | bytes 3145760 | tf_op jit(solution)/shard_map/ppermute | solution.py:8
  131.8 9.1 %fusion.28 = f32[256,384]{0,1:T(8,128)S(1)} fusion(bf16[256,8192]{1,0:T(8,128)(2,1)} %param.19, bf16[4096,384]{1,0:T(8,128)(2,1)} %maximum_select_fusion.8, bf16[4096,384]{1,0:T(8,128)(2,1)} %collective-permute-done.1, pred[]{:T(512)S(6)} %eq.17), kind=kOutput, calls=%fused_computation.45 | convolution fusion | flops 1638924288 | bytes 10878977 | tf_op jit(solution)/shard_map/dot_general | solution.py:64
  144.7 8.1 %collective-permute-done.2 = f32[256,384]{0,1:T(8,128)S(1)} collective-permute-done((f32[256,384]{0,1:T(8,128)S(1)}, f32[256,384]{0,1:T(8,128)S(1)}, u32[]{:S(2)}, u32[]{:S(2)}) %collective-permute-start.2) | collective-permute-done | bytes 393248 | tf_op jit(solution)/shard_map/ppermute | solution.py:8
  154.8 25.7 %all_gather.13 = bf16[1024,384]{1,0:T(8,128)(2,1)S(1)} all-gather(bf16[128,384]{1,0:T(8,128)(2,1)S(1)} %fusion.31), channel_id=1, replica_groups=mesh['gx'=32,'gy'=8] {'gy'}, dimensions={0}, use_global_device_ids=true | all-gather | bytes 884736 | tf_op jit(solution)/shard_map/all_gather | solution.py:29
  184.8 35.0 %collective-permute-done.4 = bf16[2048,384]{1,0:T(8,128)(2,1)S(1)} collective-permute-done((bf16[2048,384]{1,0:T(8,128)(2,1)S(1)}, bf16[2048,384]{1,0:T(8,128)(2,1)S(1)}, u32[]{:S(2)}, u32[]{:S(2)}) %collective-permute-start.4) | collective-permute-done | bytes 1572896 | tf_op jit(solution)/shard_map/ppermute | solution.py:8
  219.8 8.3 %maximum_select_fusion.9 = bf16[4096,384]{1,0:T(8,128)(2,1)} fusion(bf16[2048,384]{1,0:T(8,128)(2,1)S(1)} %maximum_select_fusion.12, bf16[2048,384]{1,0:T(8,128)(2,1)S(1)} %collective-permute-done.4, pred[]{:T(512)S(6)} %eq.17), kind=kLoop, calls=%fused_computation.39 | loop fusion | flops 14155776 | bytes 6291457 | tf_op jit(solution)/shard_map/jit(_where)/select_n | solution.py:34
  231.8 67.4 %collective-permute-done.5 = bf16[4096,384]{1,0:T(8,128)(2,1)} collective-permute-done((bf16[4096,384]{1,0:T(8,128)(2,1)}, bf16[4096,384]{1,0:T(8,128)(2,1)}, u32[]{:S(2)}, u32[]{:S(2)}) %collective-permute-start.5) | collective-permute-done | bytes 3145760 | tf_op jit(solution)/shard_map/ppermute | solution.py:8
  299.2 6.3 fusion.29
  306.4 5.1 collective-permute-done.6
  313.2 25.2 %all_gather.14 = bf16[512,384]{1,0:T(8,128)(2,1)S(1)} all-gather(bf16[64,384]{1,0:T(8,128)(2,1)S(1)} %fusion.32), channel_id=1, replica_groups=mesh['gx'=32,'gy'=8] {'gy'}, dimensions={0}, use_global_device_ids=true | all-gather | bytes 442368 | tf_op jit(solution)/shard_map/all_gather | solution.py:29
  342.0 18.1 %collective-permute-done.8 = bf16[1024,384]{1,0:T(8,128)(2,1)S(1)} collective-permute-done((bf16[1024,384]{1,0:T(8,128)(2,1)S(1)}, bf16[1024,384]{1,0:T(8,128)(2,1)S(1)}, u32[]{:S(2)}, u32[]{:S(2)}) %collective-permute-start.8) | collective-permute-done | bytes 786464 | tf_op jit(solution)/shard_map/ppermute | solution.py:8
  363.6 34.1 %collective-permute-done.9 = bf16[2048,384]{1,0:T(8,128)(2,1)S(1)} collective-permute-done((bf16[2048,384]{1,0:T(8,128)(2,1)S(1)}, bf16[2048,384]{1,0:T(8,128)(2,1)S(1)}, u32[]{:S(2)}, u32[]{:S(2)}) %collective-permute-start.9) | collective-permute-done | bytes 1572896 | tf_op jit(solution)/shard_map/ppermute | solution.py:8
  397.7 8.3 %maximum_select_fusion.10 = bf16[4096,384]{1,0:T(8,128)(2,1)} fusion(bf16[2048,384]{1,0:T(8,128)(2,1)S(1)} %maximum_select_fusion.13, bf16[2048,384]{1,0:T(8,128)(2,1)S(1)} %collective-permute-done.9, pred[]{:T(512)S(6)} %eq.16), kind=kLoop, calls=%fused_computation.40 | loop fusion | flops 14155776 | bytes 6291457 | tf_op jit(solution)/shard_map/jit(_where)/select_n | solution.py:34
  407.3 67.4 %collective-permute-done.10 = bf16[4096,384]{1,0:T(8,128)(2,1)} collective-permute-done((bf16[4096,384]{1,0:T(8,128)(2,1)}, bf16[4096,384]{1,0:T(8,128)(2,1)}, u32[]{:S(2)}, u32[]{:S(2)}) %collective-permute-start.10) | collective-permute-done | bytes 3145760 | tf_op jit(solution)/shard_map/ppermute | solution.py:8
  474.7 6.2 fusion.30
  488.5 24.8 %all_gather.15 = bf16[256,384]{1,0:T(8,128)(2,1)S(1)} all-gather(bf16[32,384]{1,0:T(8,128)(2,1)S(1)} %fusion.41), channel_id=1, replica_groups=mesh['gx'=32,'gy'=8] {'gy'}, dimensions={0}, use_global_device_ids=true | all-gather | bytes 221184 | tf_op jit(solution)/shard_map/all_gather | solution.py:29
  516.4 9.7 %collective-permute-done.13 = bf16[512,384]{1,0:T(8,128)(2,1)S(1)} collective-permute-done((bf16[512,384]{1,0:T(8,128)(2,1)S(1)}, bf16[512,384]{1,0:T(8,128)(2,1)S(1)}, u32[]{:S(2)}, u32[]{:S(2)}) %collective-permute-start.13) | collective-permute-done | bytes 393248 | tf_op jit(solution)/shard_map/ppermute | solution.py:8
  529.5 17.2 %collective-permute-done.14 = bf16[1024,384]{1,0:T(8,128)(2,1)S(1)} collective-permute-done((bf16[1024,384]{1,0:T(8,128)(2,1)S(1)}, bf16[1024,384]{1,0:T(8,128)(2,1)S(1)}, u32[]{:S(2)}, u32[]{:S(2)}) %collective-permute-start.14) | collective-permute-done | bytes 786464 | tf_op jit(solution)/shard_map/ppermute | solution.py:8
  548.1 34.1 %collective-permute-done.15 = bf16[2048,384]{1,0:T(8,128)(2,1)S(1)} collective-permute-done((bf16[2048,384]{1,0:T(8,128)(2,1)S(1)}, bf16[2048,384]{1,0:T(8,128)(2,1)S(1)}, u32[]{:S(2)}, u32[]{:S(2)}) %collective-permute-start.15) | collective-permute-done | bytes 1572896 | tf_op jit(solution)/shard_map/ppermute | solution.py:8
  582.2 7.2 %maximum_select_fusion.11 = bf16[4096,384]{1,0:T(8,128)(2,1)S(1)} fusion(bf16[2048,384]{1,0:T(8,128)(2,1)S(1)} %maximum_select_fusion.14, bf16[2048,384]{1,0:T(8,128)(2,1)S(1)} %collective-permute-done.15, pred[]{:T(512)S(6)} %eq.15), kind=kLoop, calls=%fused_computation.41 | loop fusion | flops 14155776 | bytes 6291457 | tf_op jit(solution)/shard_map/jit(_where)/select_n | solution.py:34
  591.6 66.9 %collective-permute-done.16 = bf16[4096,384]{1,0:T(8,128)(2,1)S(1)} collective-permute-done((bf16[4096,384]{1,0:T(8,128)(2,1)S(1)}, bf16[4096,384]{1,0:T(8,128)(2,1)S(1)}, u32[]{:S(2)}, u32[]{:S(2)}) %collective-permute-start.16) | collective-permute-done | bytes 3145760 | tf_op jit(solution)/shard_map/ppermute | solution.py:8
  664.7 5.1 collective-permute-done.17
  (84 shorter events, 64.1 us)
Async XLA Ops:
  7.2 292.0 %copy-start = (bf16[128,8192]{1,0:T(8,128)(2,1)S(1)}, bf16[128,8192]{1,0:T(8,128)(2,1)}, u32[]{:S(2)}) copy-start(bf16[128,8192]{1,0:T(8,128)(2,1)} %param.20) | copy-start | bytes 6291460
  7.2 44.9 %all-gather.2.cloned.1.call-start = ((), (), s32[]{:S(2)}) async-start(), calls=%async_computation | async-start | bytes 1769472 | tf_op jit(solution)/shard_map/all_gather | solution.py:29
  52.1 3.8 collective-permute-start
  61.3 70.5 %collective-permute-start.1 = (bf16[4096,384]{1,0:T(8,128)(2,1)}, bf16[4096,384]{1,0:T(8,128)(2,1)}, u32[]{:S(2)}, u32[]{:S(2)}) collective-permute-start(bf16[4096,384]{1,0:T(8,128)(2,1)} %maximum_select_fusion.8), channel_id=1, source_target_pairs={{0,16},{8,24},{16,0},{24,8},{32,48},{40,56},{48,32},{56,40},{64,80... | collective-permute-start | bytes 9437192 | tf_op jit(solution)/shard_map/ppermute | solution.py:8
  140.8 11.9 %collective-permute-start.2 = (f32[256,384]{0,1:T(8,128)S(1)}, f32[256,384]{0,1:T(8,128)S(1)}, u32[]{:S(2)}, u32[]{:S(2)}) collective-permute-start(f32[256,384]{0,1:T(8,128)S(1)} %fusion.28), channel_id=1, source_target_pairs={{0,32},{8,40},{16,48},{24,56},{32,0},{40,8},{48,16},{56,24},{64,96... | collective-permute-start | bytes 1179656 | tf_op jit(solution)/shard_map/ppermute | solution.py:8
  180.5 2.3 collective-permute-start.3
  183.2 36.5 %collective-permute-start.4 = (bf16[2048,384]{1,0:T(8,128)(2,1)S(1)}, bf16[2048,384]{1,0:T(8,128)(2,1)S(1)}, u32[]{:S(2)}, u32[]{:S(2)}) collective-permute-start(bf16[2048,384]{1,0:T(8,128)(2,1)S(1)} %maximum_select_fusion.12), channel_id=1, source_target_pairs={{0,16},{8,24},{16,0},{24,8},{32,48},{40,56},{48,32},{56,40},{64,80... | collective-permute-start | bytes 4718600 | tf_op jit(solution)/shard_map/ppermute | solution.py:8
  228.0 71.1 %collective-permute-start.5 = (bf16[4096,384]{1,0:T(8,128)(2,1)}, bf16[4096,384]{1,0:T(8,128)(2,1)}, u32[]{:S(2)}, u32[]{:S(2)}) collective-permute-start(bf16[4096,384]{1,0:T(8,128)(2,1)} %maximum_select_fusion.9), channel_id=1, source_target_pairs={{0,32},{8,40},{16,48},{24,56},{32,0},{40,8},{48,16},{56,24},{64,96... | collective-permute-start | bytes 9437192 | tf_op jit(solution)/shard_map/ppermute | solution.py:8
  305.5 5.9 collective-permute-start.6
  338.4 1.7 collective-permute-start.7
  340.4 19.7 %collective-permute-start.8 = (bf16[1024,384]{1,0:T(8,128)(2,1)S(1)}, bf16[1024,384]{1,0:T(8,128)(2,1)S(1)}, u32[]{:S(2)}, u32[]{:S(2)}) collective-permute-start(bf16[1024,384]{1,0:T(8,128)(2,1)S(1)} %maximum_select_fusion.21), channel_id=1, source_target_pairs={{0,16},{8,24},{16,0},{24,8},{32,48},{40,56},{48,32},{56,40},{64,80... | collective-permute-start | bytes 2359304 | tf_op jit(solution)/shard_map/ppermute | solution.py:8
  360.5 114.2 %copy-start.6 = (bf16[64,8192]{1,0:T(8,128)(2,1)S(1)}, bf16[64,8192]{1,0:T(8,128)(2,1)}, u32[]{:S(2)}) copy-start(bf16[64,8192]{1,0:T(8,128)(2,1)} %param.21) | copy-start | bytes 3145732
  360.5 37.2 %collective-permute-start.9 = (bf16[2048,384]{1,0:T(8,128)(2,1)S(1)}, bf16[2048,384]{1,0:T(8,128)(2,1)S(1)}, u32[]{:S(2)}, u32[]{:S(2)}) collective-permute-start(bf16[2048,384]{1,0:T(8,128)(2,1)S(1)} %maximum_select_fusion.13), channel_id=1, source_target_pairs={{0,32},{8,40},{16,48},{24,56},{32,0},{40,8},{48,16},{56,24},{64,96... | collective-permute-start | bytes 4718600 | tf_op jit(solution)/shard_map/ppermute | solution.py:8
  406.0 68.7 %collective-permute-start.10 = (bf16[4096,384]{1,0:T(8,128)(2,1)}, bf16[4096,384]{1,0:T(8,128)(2,1)}, u32[]{:S(2)}, u32[]{:S(2)}) collective-permute-start(bf16[4096,384]{1,0:T(8,128)(2,1)} %maximum_select_fusion.10), channel_id=1, source_target_pairs={{0,64},{8,72},{16,80},{24,88},{32,96},{40,104},{48,112},{56,120},{... | collective-permute-start | bytes 9437192 | tf_op jit(solution)/shard_map/ppermute | solution.py:8
  480.9 6.2 collective-permute-start.11
  513.3 1.4 collective-permute-start.12
  514.9 11.2 %collective-permute-start.13 = (bf16[512,384]{1,0:T(8,128)(2,1)S(1)}, bf16[512,384]{1,0:T(8,128)(2,1)S(1)}, u32[]{:S(2)}, u32[]{:S(2)}) collective-permute-start(bf16[512,384]{1,0:T(8,128)(2,1)S(1)} %maximum_select_fusion.23), channel_id=1, source_target_pairs={{0,16},{8,24},{16,0},{24,8},{32,48},{40,56},{48,32},{56,40},{64,80... | collective-permute-start | bytes 1179656 | tf_op jit(solution)/shard_map/ppermute | solution.py:8
  526.4 20.3 %collective-permute-start.14 = (bf16[1024,384]{1,0:T(8,128)(2,1)S(1)}, bf16[1024,384]{1,0:T(8,128)(2,1)S(1)}, u32[]{:S(2)}, u32[]{:S(2)}) collective-permute-start(bf16[1024,384]{1,0:T(8,128)(2,1)S(1)} %maximum_select_fusion.22), channel_id=1, source_target_pairs={{0,32},{8,40},{16,48},{24,56},{32,0},{40,8},{48,16},{56,24},{64,96... | collective-permute-start | bytes 2359304 | tf_op jit(solution)/shard_map/ppermute | solution.py:8
  547.2 35.0 %collective-permute-start.15 = (bf16[2048,384]{1,0:T(8,128)(2,1)S(1)}, bf16[2048,384]{1,0:T(8,128)(2,1)S(1)}, u32[]{:S(2)}, u32[]{:S(2)}) collective-permute-start(bf16[2048,384]{1,0:T(8,128)(2,1)S(1)} %maximum_select_fusion.14), channel_id=1, source_target_pairs={{0,64},{8,72},{16,80},{24,88},{32,96},{40,104},{48,112},{56,120},{... | collective-permute-start | bytes 4718600 | tf_op jit(solution)/shard_map/ppermute | solution.py:8
  589.4 69.1 %collective-permute-start.16 = (bf16[4096,384]{1,0:T(8,128)(2,1)S(1)}, bf16[4096,384]{1,0:T(8,128)(2,1)S(1)}, u32[]{:S(2)}, u32[]{:S(2)}) collective-permute-start(bf16[4096,384]{1,0:T(8,128)(2,1)S(1)} %maximum_select_fusion.11), channel_id=1, source_target_pairs={{0,128},{8,136},{16,144},{24,152},{32,160},{40,168},{48,176},{56,1... | collective-permute-start | bytes 9437192 | tf_op jit(solution)/shard_map/ppermute | solution.py:8
  660.3 4.3 collective-permute-start.18
  662.3 7.5 %collective-permute-start.17 = (f32[2,1,16,384]{3,2,1,0:T(8,128)S(1)}, f32[2,1,16,384]{3,2,1,0:T(8,128)S(1)}, u32[]{:S(2)}, u32[]{:S(2)}) collective-permute-start(f32[2,1,16,384]{3,2,1,0:T(8,128)S(1)} %get-tuple-element.27), channel_id=1, source_target_pairs={{0,8},{8,16},{16,24},{24,32},{32,40},{40,48},{48,56},{56,64},{64,7... | collective-permute-start | bytes 147464 | tf_op jit(solution)/shard_map/ppermute | solution.py:19
  669.8 5.9 collective-permute-start.20
  673.1 5.6 collective-permute-start.19
  (6 other events, 300.0 us)
Sparse Core Ops, SparseCore 0:
  9.8 42.2 all-gather.1
where the time goes:
time: 687 us; the launch traced here: 686 us
  waiting for transfers between devices  498 us (72%)
  blocking collectives  75.7 us (11%)
  starting transfers between devices  35.3 us (5%)
  other arithmetic  32.4 us (5%)
  matrix products  23.4 us (3%)
  between operations  14.4 us (2%)
  local copies, waits for them, and re-layouts  6.91 us (1%)
    ppermute x17, waiting for transfers between devices, swapped(): lax.ppermute(x, axis, [(i, i ^ 1 << distance) for i in range(lax.axis_siz...  445 us
    all_gather x3, blocking collectives, group_rows(): values = lax.all_gather(values, 'gy', axis=0, tiled=True)  75.7 us
    all_gather x1, waiting for transfers between devices, group_rows(): values = lax.all_gather(values, 'gy', axis=0, tiled=True)  44.2 us
    select_n x10, other arithmetic, group_rows(): jnp.where(upper, jnp.concatenate([other, values], 0), jnp.concatenate([va...  31.2 us
    ppermute x17, starting transfers between devices, swapped(): lax.ppermute(x, axis, [(i, i ^ 1 << distance) for i in range(lax.axis_siz...  25.1 us
    dot_general x3, matrix products, local(): product = jnp.dot(fronts[level], whole, preferred_element_type=jnp.float32)  21.6 us
  transfers between devices with their start and end apart: 22, of which 20 were waited for; matrix products, arithmetic and copies ran while one was open for 0% of the time, Pallas kernels for 0%

commit v1 on v0

--- a/solution.py
+++ b/solution.py
@@ -2,6 +2,14 @@
 import jax.numpy as jnp
 from jax import lax
 from jax.sharding import PartitionSpec as P
+
+
+def gather_by_exchange(shard, axis, dim):
+    size = lax.axis_size(axis)
+    repeats = [size if d == dim else 1 for d in range(shard.ndim)]
+    return lax.all_to_all(
+        jnp.tile(shard, repeats), axis, split_axis=dim, concat_axis=dim, tiled=True
+    )
 
 
 def swapped(x, axis, distance):
@@ -26,7 +34,7 @@
 
 
 def group_rows(values, bits):
-    values = lax.all_gather(values, "gy", axis=0, tiled=True)
+    values = gather_by_exchange(values, "gy", 0)
     column = lax.axis_index("gx")
     for bit in range(bits):
         other = swapped(values, "gx", bit)

time: 687 us -> 652 us (0.949)
  waiting for transfers between devices: 498 us -> 452 us
  blocking collectives: 75.7 us -> 98.3 us
  between operations: 14.4 us -> 1 us
    all_to_all x0 -> x4, blocking collectives: none -> 98.3 us  [gather_by_exchange(): lax.all_to_all(jnp.tile(shard, repeats), axis, split_axis=dim, concat_axi...]
    all_gather x3 -> x0, blocking collectives: 75.7 us -> none  [group_rows(): values = lax.all_gather(values, 'gy', axis=0, tiled=True)]
    all_gather x1 -> x0, waiting for transfers between devices: 44.2 us -> none  [group_rows(): values = lax.all_gather(values, 'gy', axis=0, tiled=True)]
  transfers between devices with their start and end apart: 22 -> 21, of which waited for: 20 -> 19; matrix products, arithmetic and copies ran while one was open for 0% -> 0% of each run, Pallas kernels for 0% -> 0%
where the time goes in v1:
time: 652 us
  waiting for transfers between devices  452 us (69%)
  blocking collectives  98.3 us (15%)
  starting transfers between devices  36.3 us (6%)
  other arithmetic  32.3 us (5%)
  matrix products  23.3 us (4%)
  local copies, waits for them, and re-layouts  8.24 us (1%)
    ppermute x17, waiting for transfers between devices, swapped(): lax.ppermute(x, axis, [(i, i ^ 1 << distance) for i in range(lax.axis_siz...  444 us
    all_to_all x4, blocking collectives, gather_by_exchange(): lax.all_to_all(jnp.tile(shard, repeats), axis, split_axis=dim, concat_axi...  98.3 us
    select_n x10, other arithmetic, group_rows(): jnp.where(upper, jnp.concatenate([other, values], 0), jnp.concatenate([va...  31.1 us
    ppermute x17, starting transfers between devices, swapped(): lax.ppermute(x, axis, [(i, i ^ 1 << distance) for i in range(lax.axis_siz...  26.2 us
    dot_general x3, matrix products, local(): product = jnp.dot(fronts[level], whole, preferred_element_type=jnp.float32)  21.5 us
  transfers between devices with their start and end apart: 21, of which 19 were waited for; matrix products, arithmetic and copies ran while one was open for 0% of the time, Pallas kernels for 0%

profile of v1, /device:TPU:34, one launch (start us, length us, event | category | flops | bytes accessed | tf_op | source)
XLA Modules:
  0.0 651.8 jit_solution(12825064988890354405)
XLA Ops:
  1.9 47.0 %all_to_all.36 = bf16[8,256,384]{2,1,0:T(8,128)(2,1)} all-to-all(bf16[8,256,384]{2,1,0:T(8,128)(2,1)S(1)} %tile.8), channel_id=1, replica_groups=mesh['gx'=32,'gy'=8] {'gy'}, dimensions={0} | all-to-all | bytes 3145728 | tf_op jit(solution)/shard_map/all_to_all | solution.py:10
  52.6 5.4 maximum_select_fusion.8
  59.6 68.9 %collective-permute-done.1 = bf16[4096,384]{1,0:T(8,128)(2,1)} collective-permute-done((bf16[4096,384]{1,0:T(8,128)(2,1)}, bf16[4096,384]{1,0:T(8,128)(2,1)}, u32[]{:S(2)}, u32[]{:S(2)}) %collective-permute-start.1) | collective-permute-done | bytes 3145760 | tf_op jit(solution)/shard_map/ppermute | solution.py:16
  128.5 9.0 %fusion.28 = f32[256,384]{0,1:T(8,128)S(1)} fusion(bf16[256,8192]{1,0:T(8,128)(2,1)} %param.19, bf16[4096,384]{1,0:T(8,128)(2,1)} %maximum_select_fusion.8, bf16[4096,384]{1,0:T(8,128)(2,1)} %collective-permute-done.1, pred[]{:T(512)S(6)} %eq.17), kind=kOutput, calls=%fused_computation.45 | convolution fusion | flops 1638924288 | bytes 10878977 | tf_op jit(solution)/shard_map/dot_general | solution.py:72
  141.5 7.9 %collective-permute-done.2 = f32[256,384]{0,1:T(8,128)S(1)} collective-permute-done((f32[256,384]{0,1:T(8,128)S(1)}, f32[256,384]{0,1:T(8,128)S(1)}, u32[]{:S(2)}, u32[]{:S(2)}) %collective-permute-start.2) | collective-permute-done | bytes 393248 | tf_op jit(solution)/shard_map/ppermute | solution.py:16
  151.6 24.4 %all_to_all.37 = bf16[8,128,384]{2,1,0:T(8,128)(2,1)S(1)} all-to-all(bf16[8,128,384]{2,1,0:T(8,128)(2,1)S(1)} %tile.9), channel_id=1, replica_groups=mesh['gx'=32,'gy'=8] {'gy'}, dimensions={0} | all-to-all | bytes 1572864 | tf_op jit(solution)/shard_map/all_to_all | solution.py:10
  180.3 34.9 %collective-permute-done.4 = bf16[2048,384]{1,0:T(8,128)(2,1)S(1)} collective-permute-done((bf16[2048,384]{1,0:T(8,128)(2,1)S(1)}, bf16[2048,384]{1,0:T(8,128)(2,1)S(1)}, u32[]{:S(2)}, u32[]{:S(2)}) %collective-permute-start.4) | collective-permute-done | bytes 1572896 | tf_op jit(solution)/shard_map/ppermute | solution.py:16
  215.2 8.2 %maximum_select_fusion.9 = bf16[4096,384]{1,0:T(8,128)(2,1)} fusion(bf16[2048,384]{1,0:T(8,128)(2,1)S(1)} %maximum_select_fusion.12, bf16[2048,384]{1,0:T(8,128)(2,1)S(1)} %collective-permute-done.4, pred[]{:T(512)S(6)} %eq.17), kind=kLoop, calls=%fused_computation.39 | loop fusion | flops 14155776 | bytes 6291457 | tf_op jit(solution)/shard_map/jit(_where)/select_n | solution.py:42
  227.3 67.2 %collective-permute-done.5 = bf16[4096,384]{1,0:T(8,128)(2,1)} collective-permute-done((bf16[4096,384]{1,0:T(8,128)(2,1)}, bf16[4096,384]{1,0:T(8,128)(2,1)}, u32[]{:S(2)}, u32[]{:S(2)}) %collective-permute-start.5) | collective-permute-done | bytes 3145760 | tf_op jit(solution)/shard_map/ppermute | solution.py:16
  294.5 6.3 fusion.29
  301.7 5.1 collective-permute-done.6
  308.6 14.6 %all_to_all.38 = bf16[8,64,384]{2,1,0:T(8,128)(2,1)S(1)} all-to-all(bf16[8,64,384]{2,1,0:T(8,128)(2,1)S(1)} %tile.10), channel_id=1, replica_groups=mesh['gx'=32,'gy'=8] {'gy'}, dimensions={0} | all-to-all | bytes 786432 | tf_op jit(solution)/shard_map/all_to_all | solution.py:10
  326.8 18.0 %collective-permute-done.8 = bf16[1024,384]{1,0:T(8,128)(2,1)S(1)} collective-permute-done((bf16[1024,384]{1,0:T(8,128)(2,1)S(1)}, bf16[1024,384]{1,0:T(8,128)(2,1)S(1)}, u32[]{:S(2)}, u32[]{:S(2)}) %collective-permute-start.8) | collective-permute-done | bytes 786464 | tf_op jit(solution)/shard_map/ppermute | solution.py:16
  348.6 33.9 %collective-permute-done.9 = bf16[2048,384]{1,0:T(8,128)(2,1)S(1)} collective-permute-done((bf16[2048,384]{1,0:T(8,128)(2,1)S(1)}, bf16[2048,384]{1,0:T(8,128)(2,1)S(1)}, u32[]{:S(2)}, u32[]{:S(2)}) %collective-permute-start.9) | collective-permute-done | bytes 1572896 | tf_op jit(solution)/shard_map/ppermute | solution.py:16
  382.5 8.2 %maximum_select_fusion.10 = bf16[4096,384]{1,0:T(8,128)(2,1)} fusion(bf16[2048,384]{1,0:T(8,128)(2,1)S(1)} %maximum_select_fusion.13, bf16[2048,384]{1,0:T(8,128)(2,1)S(1)} %collective-permute-done.9, pred[]{:T(512)S(6)} %eq.16), kind=kLoop, calls=%fused_computation.40 | loop fusion | flops 14155776 | bytes 6291457 | tf_op jit(solution)/shard_map/jit(_where)/select_n | solution.py:42
  392.0 67.4 %collective-permute-done.10 = bf16[4096,384]{1,0:T(8,128)(2,1)} collective-permute-done((bf16[4096,384]{1,0:T(8,128)(2,1)}, bf16[4096,384]{1,0:T(8,128)(2,1)}, u32[]{:S(2)}, u32[]{:S(2)}) %collective-permute-start.10) | collective-permute-done | bytes 3145760 | tf_op jit(solution)/shard_map/ppermute | solution.py:16
  459.5 6.2 fusion.30
  473.2 12.4 %all_to_all.39 = bf16[8,32,384]{2,1,0:T(8,128)(2,1)S(1)} all-to-all(bf16[8,32,384]{2,1,0:T(8,128)(2,1)S(1)} %tile.11), channel_id=1, replica_groups=mesh['gx'=32,'gy'=8] {'gy'}, dimensions={0} | all-to-all | bytes 393216 | tf_op jit(solution)/shard_map/all_to_all | solution.py:10
  488.8 9.6 %collective-permute-done.13 = bf16[512,384]{1,0:T(8,128)(2,1)S(1)} collective-permute-done((bf16[512,384]{1,0:T(8,128)(2,1)S(1)}, bf16[512,384]{1,0:T(8,128)(2,1)S(1)}, u32[]{:S(2)}, u32[]{:S(2)}) %collective-permute-start.13) | collective-permute-done | bytes 393248 | tf_op jit(solution)/shard_map/ppermute | solution.py:16
  502.0 17.1 %collective-permute-done.14 = bf16[1024,384]{1,0:T(8,128)(2,1)S(1)} collective-permute-done((bf16[1024,384]{1,0:T(8,128)(2,1)S(1)}, bf16[1024,384]{1,0:T(8,128)(2,1)S(1)}, u32[]{:S(2)}, u32[]{:S(2)}) %collective-permute-start.14) | collective-permute-done | bytes 786464 | tf_op jit(solution)/shard_map/ppermute | solution.py:16
  520.3 34.2 %collective-permute-done.15 = bf16[2048,384]{1,0:T(8,128)(2,1)S(1)} collective-permute-done((bf16[2048,384]{1,0:T(8,128)(2,1)S(1)}, bf16[2048,384]{1,0:T(8,128)(2,1)S(1)}, u32[]{:S(2)}, u32[]{:S(2)}) %collective-permute-start.15) | collective-permute-done | bytes 1572896 | tf_op jit(solution)/shard_map/ppermute | solution.py:16
  554.5 7.2 %maximum_select_fusion.11 = bf16[4096,384]{1,0:T(8,128)(2,1)S(1)} fusion(bf16[2048,384]{1,0:T(8,128)(2,1)S(1)} %maximum_select_fusion.14, bf16[2048,384]{1,0:T(8,128)(2,1)S(1)} %collective-permute-done.15, pred[]{:T(512)S(6)} %eq.15), kind=kLoop, calls=%fused_computation.41 | loop fusion | flops 14155776 | bytes 6291457 | tf_op jit(solution)/shard_map/jit(_where)/select_n | solution.py:42
  563.9 66.9 %collective-permute-done.16 = bf16[4096,384]{1,0:T(8,128)(2,1)S(1)} collective-permute-done((bf16[4096,384]{1,0:T(8,128)(2,1)S(1)}, bf16[4096,384]{1,0:T(8,128)(2,1)S(1)}, u32[]{:S(2)}, u32[]{:S(2)}) %collective-permute-start.16) | collective-permute-done | bytes 3145760 | tf_op jit(solution)/shard_map/ppermute | solution.py:16
  637.0 5.1 collective-permute-done.17
  (86 shorter events, 65.9 us)
Async XLA Ops:
  0.6 293.9 %copy-start = (bf16[128,8192]{1,0:T(8,128)(2,1)S(1)}, bf16[128,8192]{1,0:T(8,128)(2,1)}, u32[]{:S(2)}) copy-start(bf16[128,8192]{1,0:T(8,128)(2,1)} %param.20) | copy-start | bytes 6291460
  48.8 3.8 collective-permute-start
  58.0 70.5 %collective-permute-start.1 = (bf16[4096,384]{1,0:T(8,128)(2,1)}, bf16[4096,384]{1,0:T(8,128)(2,1)}, u32[]{:S(2)}, u32[]{:S(2)}) collective-permute-start(bf16[4096,384]{1,0:T(8,128)(2,1)} %maximum_select_fusion.8), channel_id=1, source_target_pairs={{0,16},{8,24},{16,0},{24,8},{32,48},{40,56},{48,32},{56,40},{64,80... | collective-permute-start | bytes 9437192 | tf_op jit(solution)/shard_map/ppermute | solution.py:16
  137.5 11.9 %collective-permute-start.2 = (f32[256,384]{0,1:T(8,128)S(1)}, f32[256,384]{0,1:T(8,128)S(1)}, u32[]{:S(2)}, u32[]{:S(2)}) collective-permute-start(f32[256,384]{0,1:T(8,128)S(1)} %fusion.28), channel_id=1, source_target_pairs={{0,32},{8,40},{16,48},{24,56},{32,0},{40,8},{48,16},{56,24},{64,96... | collective-permute-start | bytes 1179656 | tf_op jit(solution)/shard_map/ppermute | solution.py:16
  175.9 2.3 collective-permute-start.3
  178.6 36.5 %collective-permute-start.4 = (bf16[2048,384]{1,0:T(8,128)(2,1)S(1)}, bf16[2048,384]{1,0:T(8,128)(2,1)S(1)}, u32[]{:S(2)}, u32[]{:S(2)}) collective-permute-start(bf16[2048,384]{1,0:T(8,128)(2,1)S(1)} %maximum_select_fusion.12), channel_id=1, source_target_pairs={{0,16},{8,24},{16,0},{24,8},{32,48},{40,56},{48,32},{56,40},{64,80... | collective-permute-start | bytes 4718600 | tf_op jit(solution)/shard_map/ppermute | solution.py:16
  223.4 71.1 %collective-permute-start.5 = (bf16[4096,384]{1,0:T(8,128)(2,1)}, bf16[4096,384]{1,0:T(8,128)(2,1)}, u32[]{:S(2)}, u32[]{:S(2)}) collective-permute-start(bf16[4096,384]{1,0:T(8,128)(2,1)} %maximum_select_fusion.9), channel_id=1, source_target_pairs={{0,32},{8,40},{16,48},{24,56},{32,0},{40,8},{48,16},{56,24},{64,96... | collective-permute-start | bytes 9437192 | tf_op jit(solution)/shard_map/ppermute | solution.py:16
  300.9 5.9 collective-permute-start.6
  323.1 1.7 collective-permute-start.7
  325.2 19.7 %collective-permute-start.8 = (bf16[1024,384]{1,0:T(8,128)(2,1)S(1)}, bf16[1024,384]{1,0:T(8,128)(2,1)S(1)}, u32[]{:S(2)}, u32[]{:S(2)}) collective-permute-start(bf16[1024,384]{1,0:T(8,128)(2,1)S(1)} %maximum_select_fusion.21), channel_id=1, source_target_pairs={{0,16},{8,24},{16,0},{24,8},{32,48},{40,56},{48,32},{56,40},{64,80... | collective-permute-start | bytes 2359304 | tf_op jit(solution)/shard_map/ppermute | solution.py:16
  345.3 114.2 %copy-start.6 = (bf16[64,8192]{1,0:T(8,128)(2,1)S(1)}, bf16[64,8192]{1,0:T(8,128)(2,1)}, u32[]{:S(2)}) copy-start(bf16[64,8192]{1,0:T(8,128)(2,1)} %param.21) | copy-start | bytes 3145732
  345.3 37.2 %collective-permute-start.9 = (bf16[2048,384]{1,0:T(8,128)(2,1)S(1)}, bf16[2048,384]{1,0:T(8,128)(2,1)S(1)}, u32[]{:S(2)}, u32[]{:S(2)}) collective-permute-start(bf16[2048,384]{1,0:T(8,128)(2,1)S(1)} %maximum_select_fusion.13), channel_id=1, source_target_pairs={{0,32},{8,40},{16,48},{24,56},{32,0},{40,8},{48,16},{56,24},{64,96... | collective-permute-start | bytes 4718600 | tf_op jit(solution)/shard_map/ppermute | solution.py:16
  390.7 68.7 %collective-permute-start.10 = (bf16[4096,384]{1,0:T(8,128)(2,1)}, bf16[4096,384]{1,0:T(8,128)(2,1)}, u32[]{:S(2)}, u32[]{:S(2)}) collective-permute-start(bf16[4096,384]{1,0:T(8,128)(2,1)} %maximum_select_fusion.10), channel_id=1, source_target_pairs={{0,64},{8,72},{16,80},{24,88},{32,96},{40,104},{48,112},{56,120},{... | collective-permute-start | bytes 9437192 | tf_op jit(solution)/shard_map/ppermute | solution.py:16
  465.6 6.2 collective-permute-start.11
  485.6 1.4 collective-permute-start.12
  487.2 11.2 %collective-permute-start.13 = (bf16[512,384]{1,0:T(8,128)(2,1)S(1)}, bf16[512,384]{1,0:T(8,128)(2,1)S(1)}, u32[]{:S(2)}, u32[]{:S(2)}) collective-permute-start(bf16[512,384]{1,0:T(8,128)(2,1)S(1)} %maximum_select_fusion.23), channel_id=1, source_target_pairs={{0,16},{8,24},{16,0},{24,8},{32,48},{40,56},{48,32},{56,40},{64,80... | collective-permute-start | bytes 1179656 | tf_op jit(solution)/shard_map/ppermute | solution.py:16
  498.7 20.3 %collective-permute-start.14 = (bf16[1024,384]{1,0:T(8,128)(2,1)S(1)}, bf16[1024,384]{1,0:T(8,128)(2,1)S(1)}, u32[]{:S(2)}, u32[]{:S(2)}) collective-permute-start(bf16[1024,384]{1,0:T(8,128)(2,1)S(1)} %maximum_select_fusion.22), channel_id=1, source_target_pairs={{0,32},{8,40},{16,48},{24,56},{32,0},{40,8},{48,16},{56,24},{64,96... | collective-permute-start | bytes 2359304 | tf_op jit(solution)/shard_map/ppermute | solution.py:16
  519.5 111.3 %copy-start.7 = (bf16[32,8192]{1,0:T(8,128)(2,1)S(1)}, bf16[32,8192]{1,0:T(8,128)(2,1)}, u32[]{:S(2)}) copy-start(bf16[32,8192]{1,0:T(8,128)(2,1)} %param.22) | copy-start | bytes 1572868
  519.5 35.0 %collective-permute-start.15 = (bf16[2048,384]{1,0:T(8,128)(2,1)S(1)}, bf16[2048,384]{1,0:T(8,128)(2,1)S(1)}, u32[]{:S(2)}, u32[]{:S(2)}) collective-permute-start(bf16[2048,384]{1,0:T(8,128)(2,1)S(1)} %maximum_select_fusion.14), channel_id=1, source_target_pairs={{0,64},{8,72},{16,80},{24,88},{32,96},{40,104},{48,112},{56,120},{... | collective-permute-start | bytes 4718600 | tf_op jit(solution)/shard_map/ppermute | solution.py:16
  561.7 69.1 %collective-permute-start.16 = (bf16[4096,384]{1,0:T(8,128)(2,1)S(1)}, bf16[4096,384]{1,0:T(8,128)(2,1)S(1)}, u32[]{:S(2)}, u32[]{:S(2)}) collective-permute-start(bf16[4096,384]{1,0:T(8,128)(2,1)S(1)} %maximum_select_fusion.11), channel_id=1, source_target_pairs={{0,128},{8,136},{16,144},{24,152},{32,160},{40,168},{48,176},{56,1... | collective-permute-start | bytes 9437192 | tf_op jit(solution)/shard_map/ppermute | solution.py:16
  632.6 4.3 collective-permute-start.18
  634.6 7.5 %collective-permute-start.17 = (f32[2,1,16,384]{3,2,1,0:T(8,128)S(1)}, f32[2,1,16,384]{3,2,1,0:T(8,128)S(1)}, u32[]{:S(2)}, u32[]{:S(2)}) collective-permute-start(f32[2,1,16,384]{3,2,1,0:T(8,128)S(1)} %get-tuple-element.27), channel_id=1, source_target_pairs={{0,8},{8,16},{16,24},{24,32},{32,40},{40,48},{48,56},{56,64},{64,7... | collective-permute-start | bytes 147464 | tf_op jit(solution)/shard_map/ppermute | solution.py:27
  642.1 5.9 collective-permute-start.20
  645.5 5.6 collective-permute-start.19
  (5 other events, 188.6 us)
